TPU v7x, 256 devices: a whole 4x4x8 slice. The times are simulated.
256 devices in a mesh: member: 4 (over z_hi), token: 64 (over z_lo, x, y, core).
Axes of the slice: x: 4, y: 4, z: 8 (z_hi: 4, z_lo: 2; z = z_hi * 2 + z_lo), core: 2. Of those that a mesh axis runs over, the one named last changes fastest.
Arguments:
- members_in: bfloat16 [8, 8192, 1024], P('member', 'token'), may hold values from -16 to 16
- member_noise: bfloat16 [8, 8192, 1024], P('member', 'token'), may hold values from -6 to 6
- norm_gain: float32 [1024], replicated, may hold values from 0.25 to 1.75
- weight_query: bfloat16 [1024, 1024], replicated, may hold values from -0.1875 to 0.1875
- weight_key: bfloat16 [1024, 1024], replicated, may hold values from -0.1875 to 0.1875
- weight_value: bfloat16 [1024, 1024], replicated, may hold values from -0.1875 to 0.1875
- weight_out: bfloat16 [1024, 1024], replicated, may hold values from -0.1875 to 0.1875
- decoder_projection_weight: bfloat16 [100, 1024], replicated, may hold values from -0.1875 to 0.1875
- decoder_bias: float32 [100], replicated, may hold values from -3 to 3
- observations: float32 [100, 65536], P(None, 'token'), may hold values from -6 to 6
- surface_extent_factor: float32 [65536], P('token'), may hold values from 0.3 to 3
- quantity_scoring_factor: float32 [100], replicated, may hold values from 0.2 to 2
- point_map: int32 [65536], P('token'), may hold values from 0 to 127
Outputs:
- mean_scoring: float32 [], replicated
- grad_members: bfloat16 [8, 8192, 1024], P('member', 'token')
- grad_out: float32 [1024, 1024], P('token')
- grad_decoder: float32 [100, 1024], replicated
Inputs may be any that keep to these rules, and one draw needn't show every extreme that they name: Point p belongs to token (p // 1024) * 128 + point_map[p].
All inputs are finite; a program needn't handle non-finite values.
Results may differ from a plain program's by a relative error of at most 0.015.
Values may be sent and summed in bfloat16 or wider, within the bound.
No kernel may reach another device: no remote copies, remote signals or barrier semaphores. Data moves between devices by JAX's collectives and lax.ppermute only.
A program may use at most 128 MiB of HBM per device.

v0:
```python
import jax
import jax.numpy as jnp
from jax import lax
from jax.sharding import PartitionSpec as P

HEADS = 16
HALF = 128
EPSILON = 1e-06
SMOOTH = 0.01


def extended_2(block, sides, width):
    for axis, dim in sides:
        count = lax.axis_size(axis)
        forward = [(i, i + 1) for i in range(count - 1)]
        backward = [(target, source) for source, target in forward]
        low = lax.ppermute(
            lax.slice_in_dim(block, block.shape[dim] - width, None, axis=dim), axis, forward
        )
        high = lax.ppermute(lax.slice_in_dim(block, 0, width, axis=dim), axis, backward)
        block = jnp.concatenate([low, block, high], axis=dim)
    return block


def from_behind(block, axis, distance):
    devices = range(lax.axis_size(axis))
    route = [(i - distance, i) for i in devices if i - distance in devices]
    return lax.ppermute(block, axis, route)


def normalize_heads(flat):
    rows, width = flat.shape
    split = flat.reshape(rows, HEADS, width // HEADS)
    split = split * lax.rsqrt(jnp.mean(split * split, axis=-1, keepdims=True) + EPSILON)
    return split.reshape(rows, width)


def project(state_in, member_noise, norm_gain, weight_query, weight_key, weight_value):
    member_rows, tokens, width = state_in.shape
    mixed = state_in + member_noise.astype(jnp.float32)
    normed = (
        mixed * lax.rsqrt(jnp.mean(mixed * mixed, axis=-1, keepdims=True) + EPSILON) * norm_gain
    ).astype(jnp.bfloat16)
    flat = normed.reshape(member_rows * tokens, width)
    query = normalize_heads(jnp.dot(flat, weight_query, preferred_element_type=jnp.float32)).astype(
        jnp.bfloat16
    )
    key = normalize_heads(jnp.dot(flat, weight_key, preferred_element_type=jnp.float32)).astype(
        jnp.bfloat16
    )
    value = jnp.dot(flat, weight_value, preferred_element_type=jnp.float32).astype(jnp.bfloat16)
    full_shape = (member_rows, tokens, width)
    return (query.reshape(full_shape), key.reshape(full_shape), value.reshape(full_shape))


def attend(query, keys, values, leading_realization, total):
    member_rows, queries, width = query.shape
    realization_number = keys.shape[1]
    depth = width // HEADS
    query_heads = query.reshape(member_rows, queries, HEADS, depth)
    key_heads = keys.reshape(member_rows, realization_number, HEADS, depth)
    value_heads = values.reshape(member_rows, realization_number, HEADS, depth)
    scores = jnp.einsum(
        "mqhd,mkhd->mhqk", query_heads, key_heads, preferred_element_type=jnp.float32
    ) / jnp.sqrt(jnp.float32(depth))
    query_pos = leading_realization + lax.iota(jnp.int32, queries)
    key_pos = leading_realization - HALF + lax.iota(jnp.int32, realization_number)
    allowed = (key_pos[None, :] >= query_pos[:, None] - HALF) & (
        key_pos[None, :] < query_pos[:, None] + HALF
    )
    allowed = allowed & (key_pos[None, :] >= 0) & (key_pos[None, :] < total)
    raised = jnp.where(allowed[None, None], jnp.exp(scores), jnp.float32(0.0))
    probs = (raised / jnp.sum(raised, axis=-1, keepdims=True)).astype(jnp.bfloat16)
    mixed = jnp.einsum("mhqk,mkhd->mqhd", probs, value_heads, preferred_element_type=jnp.float32)
    return mixed.reshape(member_rows, queries, width).astype(jnp.bfloat16)


def softened_magnitude(diff):
    return jnp.sqrt(diff * diff + SMOOTH)


def unbiased_ranked_score(
    realization_prediction, observed_grid, surface_extent, quantity_scoring_factor
):
    realization_number = realization_prediction.shape[0]
    accuracy_part = softened_magnitude(realization_prediction[0] - observed_grid)
    for realization_position in range(1, realization_number):
        accuracy_part = accuracy_part + softened_magnitude(
            realization_prediction[realization_position] - observed_grid
        )
    dispersion_part = jnp.zeros_like(accuracy_part)
    for leading_realization in range(realization_number):
        for paired_realization in range(leading_realization + 1, realization_number):
            dispersion_part = dispersion_part + softened_magnitude(
                realization_prediction[leading_realization]
                - realization_prediction[paired_realization]
            )
    score = accuracy_part / realization_number - dispersion_part / (
        realization_number * (realization_number - 1)
    )
    return jnp.sum(quantity_scoring_factor[:, None] * surface_extent[None, :] * score)


def shards(
    members_in,
    member_noise,
    norm_gain,
    weight_query,
    weight_key,
    weight_value,
    weight_out,
    decoder_projection_weight,
    decoder_bias,
    observations,
    surface_extent_factor,
    quantity_scoring_factor,
    point_map,
):
    member_rows, tokens, width = members_in.shape
    state = members_in.astype(jnp.float32)

    def front(state_in):
        return project(state_in, member_noise, norm_gain, weight_query, weight_key, weight_value)

    (query, key, value), front_pull = jax.vjp(front, state)
    stacked = jnp.stack([key, value])
    extended = extended_2(stacked, (("token", 2),), HALF)
    leading_realization = lax.axis_index("token") * tokens
    total = tokens * lax.axis_size("token")

    def middle(query_in, extended_in):
        return attend(query_in, extended_in[0], extended_in[1], leading_realization, total)

    attended, middle_pull = jax.vjp(middle, query, extended)
    flat_att = attended.reshape(member_rows * tokens, width)
    update = jnp.dot(flat_att, weight_out, preferred_element_type=jnp.float32).reshape(
        member_rows, tokens, width
    )
    residual_stream_state = (state + member_noise.astype(jnp.float32) + update).astype(jnp.bfloat16)

    def decode_tokens(residual_in, decoder_in):
        mapping_array = jnp.einsum(
            "vc,mtc->mvt",
            decoder_in.astype(jnp.bfloat16),
            residual_in,
            preferred_element_type=jnp.float32,
        )
        mapping_array = mapping_array + decoder_bias[None, :, None]
        return jnp.take(mapping_array, point_map, axis=2)

    realization_prediction, readout_slope_pulled = jax.vjp(
        decode_tokens, residual_stream_state, decoder_projection_weight.astype(jnp.float32)
    )
    location_places = realization_prediction.shape[2]
    groups = lax.axis_size("member")
    local_shard = lax.axis_index("member")
    gathered_lines = lax.all_gather(realization_prediction, "member", axis=0, tiled=True)

    def score_all(whole):
        return unbiased_ranked_score(
            whole, observations, surface_extent_factor, quantity_scoring_factor
        )

    full_loss, score_pull = jax.vjp(score_all, gathered_lines)
    (complete_gradient,) = score_pull(jnp.ones((), jnp.float32))
    prediction_slope = lax.dynamic_slice_in_dim(
        complete_gradient, local_shard * member_rows, member_rows, 0
    )
    partial_loss = full_loss / groups
    carried_slope, readout_piece_result = readout_slope_pulled(prediction_slope)
    overall_scoring_amount, grad_decoder = lax.psum(
        (partial_loss, readout_piece_result), ("member", "token")
    )
    mean_scoring = overall_scoring_amount / (
        realization_prediction.shape[1] * location_places * lax.axis_size("token")
    )
    flat_grad = carried_slope.reshape(member_rows * tokens, width)
    grad_attended = (
        jnp.dot(flat_grad, weight_out.T, preferred_element_type=jnp.float32)
        .astype(jnp.bfloat16)
        .reshape(member_rows, tokens, width)
    )
    grad_query, grad_extended = middle_pull(grad_attended)
    lower_rim = grad_extended[:, :, :HALF]
    upper_rim = grad_extended[:, :, tokens + HALF :]
    inner = grad_extended[:, :, HALF : tokens + HALF].astype(jnp.float32)
    from_next = from_behind(lower_rim, "token", -1)
    from_prev = from_behind(upper_rim, "token", 1)
    inner = inner.at[:, :, tokens - HALF :].add(from_next.astype(jnp.float32))
    inner = inner.at[:, :, :HALF].add(from_prev.astype(jnp.float32))
    (grad_front,) = front_pull(
        (grad_query, inner[0].astype(jnp.bfloat16), inner[1].astype(jnp.bfloat16))
    )
    grad_members = (grad_front + carried_slope.astype(jnp.float32)).astype(jnp.bfloat16)
    contract = (((0,), (0,)), ((), ()))
    product = lax.dot_general(flat_att, flat_grad, contract, preferred_element_type=jnp.float32)
    summed = lax.psum(product.astype(jnp.bfloat16), "member").astype(jnp.float32)
    grad_out = lax.psum_scatter(summed, "token", scatter_dimension=0, tiled=True)
    return (mean_scoring, grad_members, grad_out, grad_decoder)


def solution(mesh):
    return jax.shard_map(
        shards,
        mesh=mesh,
        in_specs=(
            P("member", "token", None),
            P("member", "token", None),
            P(),
            P(),
            P(),
            P(),
            P(),
            P(),
            P(),
            P(None, "token"),
            P("token"),
            P(),
            P("token"),
        ),
        out_specs=(P(), P("member", "token", None), P("token", None), P()),
        check_vma=False,
    )
```

profile of v0, /device:TPU:64, one launch (start us, length us, event | category | flops | bytes accessed | tf_op | source)
XLA Modules:
  0.0 912.2 jit_solution(12834779146447870691)
XLA Ops:
  7.3 1.6 multiply_reduce_fusion.3
  8.9 3.9 copy.95
  13.0 0.8 copy-done.26
  13.8 2.3 multiply_reduce_fusion.2
  17.4 0.9 multiply_convert_fusion.1
  18.3 2.0 convert_element_type.154
  20.3 3.3 convolution_convert_fusion.8
  23.5 2.0 copy.96
  25.5 3.8 pad_maximum_fusion.1
  29.3 2.8 collective-permute-start
  32.1 1.6 collective-permute-start.1
  33.7 3.9 copy.98
  37.7 2.6 multiply_reduce_fusion.1
  40.9 5.7 pad_maximum_fusion
  46.5 2.2 fusion.223
  49.2 1.8 fusion.7
  51.1 1.3 divide_convert_fusion
  52.4 1.3 copy-done.11
  53.7 1.5 convolution_convert_fusion.5
  56.0 0.8 copy-done.17
  56.8 0.9 fusion.22
  57.8 1.0 copy.102
  58.8 7.5 gather_fusion
  66.3 6.1 select_bitcast_fusion
  72.4 2.3 copy.103
  75.3 85.9 %all-gather.2.cloned.1.call-done = f32[8,100,1024]{2,1,0:T(8,128)} async-done(((f32[2,100,1024]{2,1,0:T(8,128)}), f32[8,100,1024]{2,1,0:T(8,128)}) %all-gather.2.cloned.1.call-update) | async-done | bytes 3276816 | tf_op jit(solution)/shard_map/all_gather | solution.py:157
  161.2 3.2 fusion.195
  164.4 1.3 fusion.196
  165.7 1.1 fusion.197
  167.8 6.7 fusion.57
  174.5 3.5 pad_add_fusion
  178.0 1.4 fusion.37
  179.4 2.2 copy.104
  181.7 63.8 %scatter_fusion = f32[2,100,128]{1,0,2:T(2,128)S(1)} fusion(f32[2,100,128]{1,0,2:T(2,128)S(1)} %broadcast_in_dim.59, s32[1024]{0:T(1024)S(1)} %get-tuple-element.163, f32[1024,2,100]{2,1,0:T(2,128)} %copy.104), kind=kCustom, calls=%fused_computation.1 | custom fusion | flops 204800 | bytes 2461696 | tf_op jit(solution)/shard_map/transpose(jvp(jit(_take)))/scatter-add | solution.py:149
  246.0 0.8 copy-done.15
  246.8 3.2 bitcast_convert_fusion
  250.0 2.0 fusion.21
  252.3 95.8 %all-reduce.69.cloned.1.call-done = bf16[1024,1024]{1,0:T(8,128)(2,1)} async-done(((bf16[1024,1024]{1,0:T(8,128)(2,1)}), bf16[1024,1024]{1,0:T(8,128)(2,1)}) %all-reduce.69.cloned.1.call-update) | async-done | bytes 2097168 | tf_op jit(solution)/shard_map/psum | solution.py:197
  348.1 4.1 convert_element_type.189
  353.0 2.6 convolution_convert_fusion.7
  355.5 1.2 copy.106
  356.9 5.8 fusion.5
  362.8 5.8 convolution_convert_fusion.2
  368.6 1.6 copy.111
  371.2 1.6 copy.108
  372.8 1.1 copy-done.5
  373.9 3.0 fusion.23
  376.9 1.3 collective-permute-start.2
  378.2 4.2 collective-permute-start.3
  383.1 7.9 fusion.17
  391.0 79.1 %psum.21 = f32[]{:T(128)} all-reduce(f32[]{:T(128)S(6)} %div.254), channel_id=1, replica_groups=mesh['member'=4,'token'=64] {'member','token'}, use_global_device_ids=true, to_apply=%region_5.6 | all-reduce | flops 1 | bytes 8 | tf_op jit(solution)/shard_map/psum | solution.py:171
  470.7 1.8 fusion.27
  472.6 1.9 add_add_fusion.1
  474.4 1.6 fusion.224
  476.0 3.2 add_convert_fusion
  479.3 1.9 slice_convert_fusion
  481.1 2.1 reshape.877
  484.3 0.7 copy-done.45
  485.0 0.8 convolution_convert_fusion.6
  485.8 0.8 fusion.19
  486.9 1.2 fusion.26
  488.1 113.7 %all-reduce.71.cloned.1.call-done = f32[100,1024]{1,0:T(8,128)} async-done(((f32[100,1024]{1,0:T(8,128)}), f32[100,1024]{1,0:T(8,128)}) %all-reduce.71.cloned.1.call-update) | async-done | bytes 409616 | tf_op jit(solution)/shard_map/psum | solution.py:171
  601.8 300.7 %reduce-scatter.2.cloned.1.call-done = f32[16,1024]{1,0:T(8,128)} async-done(((f32[1024,1024]{1,0:T(8,128)}), f32[16,1024]{1,0:T(8,128)}) %reduce-scatter.2.cloned.1.call-update) | async-done | bytes 65552 | tf_op jit(solution)/shard_map/reduce_scatter | solution.py:198
  902.5 1.8 copy.143
  (129 shorter events, 8.8 us)
Async XLA Ops:
  7.2 48.1 %copy-start = (bf16[1024,1024]{1,0:T(8,128)(2,1)S(1)}, bf16[1024,1024]{1,0:T(8,128)(2,1)}, u32[]{:S(2)}) copy-start(bf16[1024,1024]{1,0:T(8,128)(2,1)} %param.27) | copy-start | bytes 6291460
  7.2 5.6 copy-start.8
  7.2 5.6 copy-start.7
  7.2 5.6 copy-start.41
  7.2 154.0 %all-gather.2.cloned.1.call-start = ((), (), s32[]{:S(2)}) async-start(), calls=%async_computation.1 | async-start | bytes 4259840 | tf_op jit(solution)/shard_map/all_gather | solution.py:157
  13.0 0.8 copy-start.26
  16.2 0.6 copy-start.35
  16.2 1.0 copy-start.9
  16.8 0.6 copy-start.30
  25.5 12.1 %copy-start.42 = (s32[1024]{0:T(1024)S(1)}, s32[1024]{0:T(1024)}, u32[]{:S(2)}) copy-start(s32[1024]{0:T(1024)} %param.33) | copy-start | bytes 12292
  29.3 11.2 %collective-permute-start = (bf16[2,2,128,1024]{2,1,3,0:T(2,128)(2,1)}, bf16[2,2,128,1024]{2,1,3,0:T(2,128)(2,1)}, u32[]{:S(2)}, u32[]{:S(2)}) collective-permute-start(bf16[2,2,128,1024]{2,1,3,0:T(2,128)(2,1)} %pad_maximum_fusion.1), channel_id=1, source_target_pairs={{0,1},{1,2},{2,3},{3,4},{4,5},{5,6},{6,7},{7,8},{8,9},{9,10},{10,1... | collective-permute-start | bytes 3145736 | tf_op jit(solution)/shard_map/ppermute | solution.py:17
  32.1 8.4 collective-permute-start.1
  37.6 3.2 copy-start.13
  37.6 3.2 copy-start.14
  40.3 0.6 copy-start.37
  40.3 8.9 copy-start.19
  40.3 8.9 copy-start.39
  40.4 10.6 %copy-start.28 = (pred[128,384]{1,0:T(8,128)(4,1)}, pred[128,384]{1,0:T(8,128)(4,1)S(1)}, u32[]{:S(2)}) copy-start(pred[128,384]{1,0:T(8,128)(4,1)S(1)} %and_and_fusion) | copy-start | bytes 147460
  49.0 2.0 copy-start.23
  49.2 4.5 copy-start.12
  51.0 2.7 copy-start.11
  51.0 2.7 copy-start.33
  53.7 2.3 copy-start.3
  55.2 0.8 copy-start.18
  55.2 1.6 copy-start.24
  55.2 1.6 copy-start.44
  56.0 0.8 copy-start.17
  57.8 103.4 %copy-start.32 = (f32[1024]{0:T(1024)S(1)}, f32[1024]{0:T(1024)}, u32[]{:S(2)}) copy-start(f32[1024]{0:T(1024)} %param.31) | copy-start | bytes 12292
  57.8 103.4 %copy-start.43 = (f32[100]{0:T(128)S(1)}, f32[100]{0:T(128)}, u32[]{:S(2)}) copy-start(f32[100]{0:T(128)} %param.32) | copy-start | bytes 1204
  74.7 273.4 %all-reduce.69.cloned.1.call-start = ((), (), s32[]{:S(2)}) async-start(), calls=%async_computation.2 | async-start | bytes 4194304 | tf_op jit(solution)/shard_map/psum | solution.py:197
  161.2 3.2 copy-start.2
  166.8 1.0 copy-start.27
  246.0 0.8 copy-start.15
  250.0 351.8 %all-reduce.71.cloned.1.call-start = ((), (), s32[]{:S(2)}) async-start(), calls=%async_computation.4 | async-start | bytes 851968 | tf_op jit(solution)/shard_map/psum | solution.py:171
  252.1 650.4 %reduce-scatter.2.cloned.1.call-start = ((), (), s32[]{:S(2)}) async-start(), calls=%async_computation.3 | async-start | bytes 4259840 | tf_op jit(solution)/shard_map/reduce_scatter | solution.py:198
  352.2 0.7 copy-start.34
  352.9 4.0 copy-start.29
  356.9 5.8 copy-start.20
  356.9 5.8 copy-start.40
  362.7 5.8 copy-start.47
  368.6 1.9 copy-start.4
  372.8 1.2 copy-start.5
  376.9 99.1 %collective-permute-start.2 = (bf16[2,2,128,1024]{2,1,3,0:T(2,128)(2,1)}, bf16[2,2,128,1024]{2,1,3,0:T(2,128)(2,1)}, u32[]{:S(2)}, u32[]{:S(2)}) collective-permute-start(bf16[2,2,128,1024]{2,1,3,0:T(2,128)(2,1)} %get-tuple-element.157), channel_id=1, source_target_pairs={{1,0},{2,1},{3,2},{4,3},{5,4},{6,5},{7,6},{8,7},{9,8},{10,9},{11,1... | collective-permute-start | bytes 3145736 | tf_op jit(solution)/shard_map/ppermute | solution.py:28
  378.2 97.8 %collective-permute-start.3 = (bf16[2,2,128,1024]{2,1,3,0:T(2,128)(2,1)}, bf16[2,2,128,1024]{2,1,3,0:T(2,128)(2,1)}, u32[]{:S(2)}, u32[]{:S(2)}) collective-permute-start(bf16[2,2,128,1024]{2,1,3,0:T(2,128)(2,1)} %get-tuple-element.158), channel_id=1, source_target_pairs={{0,1},{1,2},{2,3},{3,4},{4,5},{5,6},{6,7},{7,8},{8,9},{9,10},{10,1... | collective-permute-start | bytes 3145736 | tf_op jit(solution)/shard_map/ppermute | solution.py:28
  383.0 89.5 %copy-start.38 = (f32[256,16]{0,1:T(8,128)S(1)}, f32[256,16]{0,1:T(8,128)}, u32[]{:S(2)}) copy-start(f32[256,16]{0,1:T(8,128)} %copy-done.37) | copy-start | bytes 49156
  470.7 3.8 copy-start.21
  472.5 3.5 copy-start.6
  479.3 4.0 copy-start.10
  479.3 4.1 copy-start.36
  479.3 4.2 copy-start.31
  483.2 1.0 copy-start.25
  483.2 1.8 copy-start.45
  483.4 2.4 copy-start.22
  483.4 2.4 copy-start.46
  485.8 1.2 copy-start.16
  485.8 418.5 %copy-start.1 = (bf16[1024,1024]{1,0:T(8,128)(2,1)S(1)}, bf16[1024,1024]{1,0:T(8,128)(2,1)}, u32[]{:S(2)}) copy-start(bf16[1024,1024]{1,0:T(8,128)(2,1)} %param.27) | copy-start | bytes 6291460
Sparse Core Ops, SparseCore 0:
  74.8 86.3 all-gather.1
  250.1 97.9 all-reduce.68
  354.2 247.5 all-reduce.70
  604.7 297.7 reduce-scatter.1
where the time goes:
time: 922 us; the launch traced here: 912 us
  waiting for transfers between devices  596 us (65%)
  other arithmetic  119 us (13%)
  blocking collectives  79.1 us (9%)
  local copies, waits for them, and re-layouts  45.2 us (5%)
  matrix products  44.6 us (5%)
  between operations  17.3 us (2%)
  starting transfers between devices  10.7 us (1%)
    reduce_scatter x1, waiting for transfers between devices, shards(): lax.psum_scatter(summed, 'token', scatter_dimension=0, tiled=True)  301 us
    psum x1, waiting for transfers between devices, shards(): lax.psum((partial_loss, readout_piece_result), ('member', 'token'))  114 us
    psum x1, waiting for transfers between devices, shards(): lax.psum(product.astype(jnp.bfloat16), 'member').astype(jnp.float32)  95.8 us
    all_gather x1, waiting for transfers between devices, shards(): lax.all_gather(realization_prediction, 'member', axis=0, tiled=True)  85.9 us
    psum x1, blocking collectives, shards(): lax.psum((partial_loss, readout_piece_result), ('member', 'token'))  79.1 us
    scatter-add x1, other arithmetic, decode_tokens(): return jnp.take(mapping_array, point_map, axis=2)  63.8 us
    unnamed x99, local copies, waits for them, and re-layouts  18.8 us
  transfers between devices with their start and end apart: 8, of which 4 were waited for; matrix products, arithmetic and copies ran while one was open for 6% of the time, Pallas kernels for 0%

commit v1 on v0

--- a/solution.py
+++ b/solution.py
@@ -194,7 +194,9 @@
     grad_members = (grad_front + carried_slope.astype(jnp.float32)).astype(jnp.bfloat16)
     contract = (((0,), (0,)), ((), ()))
     product = lax.dot_general(flat_att, flat_grad, contract, preferred_element_type=jnp.float32)
-    summed = lax.psum(product.astype(jnp.bfloat16), "member").astype(jnp.float32)
+    summed = jnp.sum(lax.all_gather(product.astype(jnp.bfloat16), "member"), axis=0).astype(
+        jnp.float32
+    )
     grad_out = lax.psum_scatter(summed, "token", scatter_dimension=0, tiled=True)
     return (mean_scoring, grad_members, grad_out, grad_decoder)
 

time: 922 us -> 979 us (1.062)
  waiting for transfers between devices: 596 us -> 645 us
    all_gather x0 -> x1, waiting for transfers between devices: none -> 151 us  [shards(): lax.all_gather(product.astype(jnp.bfloat16), 'member')]
    psum x1 -> x0, waiting for transfers between devices: 95.8 us -> none  [shards(): lax.psum(product.astype(jnp.bfloat16), 'member').astype(jnp.float32)]
  transfers between devices with their start and end apart: 8 -> 8, of which waited for: 4 -> 4; matrix products, arithmetic and copies ran while one was open for 6% -> 7% of each run, Pallas kernels for 0% -> 0%
where the time goes in v1:
time: 979 us; the launch traced here: 968 us
  waiting for transfers between devices  645 us (66%)
  other arithmetic  127 us (13%)
  blocking collectives  79.1 us (8%)
  local copies, waits for them, and re-layouts  45.2 us (5%)
  matrix products  44.4 us (5%)
  between operations  17.5 us (2%)
  starting transfers between devices  10.5 us (1%)
    reduce_scatter x1, waiting for transfers between devices, shards(): lax.psum_scatter(summed, 'token', scatter_dimension=0, tiled=True)  301 us
    all_gather x1, waiting for transfers between devices, shards(): lax.all_gather(product.astype(jnp.bfloat16), 'member')  151 us
    psum x1, waiting for transfers between devices, shards(): lax.psum((partial_loss, readout_piece_result), ('member', 'token'))  107 us
    all_gather x1, waiting for transfers between devices, shards(): lax.all_gather(realization_prediction, 'member', axis=0, tiled=True)  86.1 us
    psum x1, blocking collectives, shards(): lax.psum((partial_loss, readout_piece_result), ('member', 'token'))  79.1 us
    scatter-add x1, other arithmetic, decode_tokens(): return jnp.take(mapping_array, point_map, axis=2)  63.8 us
  transfers between devices with their start and end apart: 8, of which 4 were waited for; matrix products, arithmetic and copies ran while one was open for 7% of the time, Pallas kernels for 0%

profile of v1, /device:TPU:64, one launch (start us, length us, event | category | flops | bytes accessed | tf_op | source)
XLA Modules:
  0.0 968.2 jit_solution(137288566379145817)
XLA Ops:
  7.3 1.6 multiply_reduce_fusion.3
  8.9 3.9 copy.95
  13.0 0.8 copy-done.26
  13.8 2.3 multiply_reduce_fusion.2
  17.4 0.9 multiply_convert_fusion.1
  18.3 1.9 convert_element_type.156
  20.2 3.3 convolution_convert_fusion.8
  23.5 2.0 copy.96
  25.5 3.8 pad_maximum_fusion.1
  29.3 2.7 collective-permute-start
  32.0 1.8 collective-permute-start.1
  33.9 3.9 copy.98
  37.9 2.6 multiply_reduce_fusion.1
  41.1 5.7 pad_maximum_fusion
  46.8 2.2 fusion.223
  49.4 1.8 fusion.7
  51.3 1.3 divide_convert_fusion
  52.6 1.3 copy-done.11
  54.0 1.5 convolution_convert_fusion.5
  56.3 0.8 copy-done.17
  57.1 0.9 fusion.22
  58.1 1.0 copy.102
  59.1 7.4 gather_fusion
  66.5 6.1 select_bitcast_fusion
  72.6 2.3 copy.103
  75.2 86.1 %all-gather.4.cloned.1.call-done = f32[8,100,1024]{2,1,0:T(8,128)} async-done(((f32[2,100,1024]{2,1,0:T(8,128)}), f32[8,100,1024]{2,1,0:T(8,128)}) %all-gather.4.cloned.1.call-update) | async-done | bytes 3276816 | tf_op jit(solution)/shard_map/all_gather | solution.py:157
  161.2 3.2 fusion.195
  164.4 1.3 fusion.196
  165.7 1.1 fusion.197
  167.8 6.7 fusion.57
  174.5 3.5 pad_add_fusion
  178.1 1.4 fusion.37
  179.4 2.2 copy.104
  181.7 63.8 %scatter_fusion = f32[2,100,128]{1,0,2:T(2,128)S(1)} fusion(f32[2,100,128]{1,0,2:T(2,128)S(1)} %broadcast_in_dim.59, s32[1024]{0:T(1024)S(1)} %get-tuple-element.163, f32[1024,2,100]{2,1,0:T(2,128)} %copy.104), kind=kCustom, calls=%fused_computation.1 | custom fusion | flops 204800 | bytes 2461696 | tf_op jit(solution)/shard_map/transpose(jvp(jit(_take)))/scatter-add | solution.py:149
  246.0 0.8 copy-done.15
  246.8 3.1 bitcast_convert_fusion
  249.9 2.0 fusion.21
  252.2 151.1 %all-gather.6.cloned.1.call-done = bf16[4096,1024]{1,0:T(8,128)(2,1)} async-done(((bf16[1024,1024]{1,0:T(8,128)(2,1)}), bf16[4096,1024]{1,0:T(8,128)(2,1)}) %all-gather.6.cloned.1.call-update) | async-done | bytes 8388624 | tf_op jit(solution)/shard_map/all_gather | solution.py:197
  403.3 7.4 reduce_sum.118
  410.8 4.0 convert_element_type.191
  415.5 2.6 convolution_convert_fusion.7
  418.1 1.2 copy.106
  419.5 5.8 fusion.5
  425.3 5.7 convolution_convert_fusion.2
  431.1 1.6 copy.111
  433.7 1.6 copy.108
  435.3 1.2 copy-done.5
  436.5 2.9 fusion.23
  439.4 1.3 collective-permute-start.2
  440.7 4.1 collective-permute-start.3
  445.5 7.9 fusion.17
  453.3 79.1 %psum.14 = f32[]{:T(128)} all-reduce(f32[]{:T(128)S(6)} %div.254), channel_id=1, replica_groups=mesh['member'=4,'token'=64] {'member','token'}, use_global_device_ids=true, to_apply=%region_5.6 | all-reduce | flops 1 | bytes 8 | tf_op jit(solution)/shard_map/psum | solution.py:171
  533.1 1.8 fusion.27
  535.0 1.9 add_add_fusion.1
  536.8 1.6 fusion.224
  538.4 3.2 add_convert_fusion
  541.7 1.9 slice_convert_fusion
  543.6 2.1 reshape.877
  547.4 0.8 convolution_convert_fusion.6
  548.2 0.8 fusion.19
  549.4 1.2 fusion.26
  550.6 107.0 %all-reduce.68.cloned.1.call-done = f32[100,1024]{1,0:T(8,128)} async-done(((f32[100,1024]{1,0:T(8,128)}), f32[100,1024]{1,0:T(8,128)}) %all-reduce.68.cloned.1.call-update) | async-done | bytes 409616 | tf_op jit(solution)/shard_map/psum | solution.py:171
  657.6 300.7 %reduce-scatter.2.cloned.1.call-done = f32[16,1024]{1,0:T(8,128)} async-done(((f32[1024,1024]{1,0:T(8,128)}), f32[16,1024]{1,0:T(8,128)}) %reduce-scatter.2.cloned.1.call-update) | async-done | bytes 65552 | tf_op jit(solution)/shard_map/reduce_scatter | solution.py:200
  958.3 1.8 copy.142
  (130 shorter events, 9.2 us)
Async XLA Ops:
  7.2 48.3 %copy-start = (bf16[1024,1024]{1,0:T(8,128)(2,1)S(1)}, bf16[1024,1024]{1,0:T(8,128)(2,1)}, u32[]{:S(2)}) copy-start(bf16[1024,1024]{1,0:T(8,128)(2,1)} %param.27) | copy-start | bytes 6291460
  7.2 5.6 copy-start.8
  7.2 5.6 copy-start.7
  7.2 5.6 copy-start.41
  7.2 154.0 %all-gather.4.cloned.1.call-start = ((), (), s32[]{:S(2)}) async-start(), calls=%async_computation.1 | async-start | bytes 4259840 | tf_op jit(solution)/shard_map/all_gather | solution.py:157
  13.0 0.8 copy-start.26
  16.2 0.6 copy-start.35
  16.2 1.0 copy-start.9
  16.8 0.6 copy-start.30
  25.5 12.3 %copy-start.42 = (s32[1024]{0:T(1024)S(1)}, s32[1024]{0:T(1024)}, u32[]{:S(2)}) copy-start(s32[1024]{0:T(1024)} %param.33) | copy-start | bytes 12292
  29.3 11.3 %collective-permute-start = (bf16[2,2,128,1024]{2,1,3,0:T(2,128)(2,1)}, bf16[2,2,128,1024]{2,1,3,0:T(2,128)(2,1)}, u32[]{:S(2)}, u32[]{:S(2)}) collective-permute-start(bf16[2,2,128,1024]{2,1,3,0:T(2,128)(2,1)} %pad_maximum_fusion.1), channel_id=1, source_target_pairs={{0,1},{1,2},{2,3},{3,4},{4,5},{5,6},{6,7},{7,8},{8,9},{9,10},{10,1... | collective-permute-start | bytes 3145736 | tf_op jit(solution)/shard_map/ppermute | solution.py:17
  32.0 8.6 collective-permute-start.1
  37.8 3.2 copy-start.13
  37.8 3.2 copy-start.14
  40.5 0.6 copy-start.37
  40.5 8.9 copy-start.19
  40.5 8.9 copy-start.39
  40.7 10.6 %copy-start.28 = (pred[128,384]{1,0:T(8,128)(4,1)}, pred[128,384]{1,0:T(8,128)(4,1)S(1)}, u32[]{:S(2)}) copy-start(pred[128,384]{1,0:T(8,128)(4,1)S(1)} %and_and_fusion) | copy-start | bytes 147460
  49.2 2.1 copy-start.23
  49.4 4.5 copy-start.12
  51.3 2.7 copy-start.11
  51.3 2.7 copy-start.33
  54.0 2.3 copy-start.3
  55.5 0.8 copy-start.18
  55.5 1.6 copy-start.24
  55.5 1.6 copy-start.44
  56.3 0.8 copy-start.17
  58.1 103.2 %copy-start.32 = (f32[1024]{0:T(1024)S(1)}, f32[1024]{0:T(1024)}, u32[]{:S(2)}) copy-start(f32[1024]{0:T(1024)} %param.31) | copy-start | bytes 12292
  58.1 103.2 %copy-start.43 = (f32[100]{0:T(128)S(1)}, f32[100]{0:T(128)}, u32[]{:S(2)}) copy-start(f32[100]{0:T(128)} %param.32) | copy-start | bytes 1204
  74.9 328.4 %all-gather.6.cloned.1.call-start = ((), (), s32[]{:S(2)}) async-start(), calls=%async_computation.4 | async-start | bytes 10485760 | tf_op jit(solution)/shard_map/all_gather | solution.py:197
  161.2 3.2 copy-start.2
  166.8 1.0 copy-start.27
  246.0 0.8 copy-start.15
  249.9 407.7 %all-reduce.68.cloned.1.call-start = ((), (), s32[]{:S(2)}) async-start(), calls=%async_computation.3 | async-start | bytes 851968 | tf_op jit(solution)/shard_map/psum | solution.py:171
  252.0 706.3 %reduce-scatter.2.cloned.1.call-start = ((), (), s32[]{:S(2)}) async-start(), calls=%async_computation.2 | async-start | bytes 4259840 | tf_op jit(solution)/shard_map/reduce_scatter | solution.py:200
  414.8 0.7 copy-start.34
  415.5 4.0 copy-start.29
  419.5 5.8 copy-start.20
  419.5 5.8 copy-start.40
  425.3 5.8 copy-start.47
  431.1 1.9 copy-start.4
  435.3 1.2 copy-start.5
  439.4 99.0 %collective-permute-start.2 = (bf16[2,2,128,1024]{2,1,3,0:T(2,128)(2,1)}, bf16[2,2,128,1024]{2,1,3,0:T(2,128)(2,1)}, u32[]{:S(2)}, u32[]{:S(2)}) collective-permute-start(bf16[2,2,128,1024]{2,1,3,0:T(2,128)(2,1)} %get-tuple-element.157), channel_id=1, source_target_pairs={{1,0},{2,1},{3,2},{4,3},{5,4},{6,5},{7,6},{8,7},{9,8},{10,9},{11,1... | collective-permute-start | bytes 3145736 | tf_op jit(solution)/shard_map/ppermute | solution.py:28
  440.7 97.7 %collective-permute-start.3 = (bf16[2,2,128,1024]{2,1,3,0:T(2,128)(2,1)}, bf16[2,2,128,1024]{2,1,3,0:T(2,128)(2,1)}, u32[]{:S(2)}, u32[]{:S(2)}) collective-permute-start(bf16[2,2,128,1024]{2,1,3,0:T(2,128)(2,1)} %get-tuple-element.158), channel_id=1, source_target_pairs={{0,1},{1,2},{2,3},{3,4},{4,5},{5,6},{6,7},{7,8},{8,9},{9,10},{10,1... | collective-permute-start | bytes 3145736 | tf_op jit(solution)/shard_map/ppermute | solution.py:28
  445.4 89.5 %copy-start.38 = (f32[256,16]{0,1:T(8,128)S(1)}, f32[256,16]{0,1:T(8,128)}, u32[]{:S(2)}) copy-start(f32[256,16]{0,1:T(8,128)} %copy-done.37) | copy-start | bytes 49156
  533.1 3.8 copy-start.21
  534.9 3.5 copy-start.6
  541.7 4.0 copy-start.10
  541.7 4.2 copy-start.36
  541.7 4.2 copy-start.31
  545.7 1.0 copy-start.25
  545.7 1.8 copy-start.45
  545.8 2.4 copy-start.22
  545.9 2.4 copy-start.46
  548.2 1.2 copy-start.16
  548.2 411.8 %copy-start.1 = (bf16[1024,1024]{1,0:T(8,128)(2,1)S(1)}, bf16[1024,1024]{1,0:T(8,128)(2,1)}, u32[]{:S(2)}) copy-start(bf16[1024,1024]{1,0:T(8,128)(2,1)} %param.27) | copy-start | bytes 6291460
Sparse Core Ops, SparseCore 0:
  75.1 86.1 all-gather.3
  250.0 153.2 all-gather.5
  409.4 248.1 all-reduce.67
  660.5 297.7 reduce-scatter.1
